TPU v7x, 32 devices: a whole 2x2x4 slice. The times are simulated.
32 devices in a mesh: seq: 8 (over y, x, core), head: 4 (over z).
Axes of the slice: x: 2, y: 2, z: 4, core: 2. Of those that a mesh axis runs over, the one named last changes fastest.
Arguments:
- tokens: bfloat16 [4096, 5376], P('seq', 'head'), may hold values from -32 to 32
- query_weight: bfloat16 [5376, 4096], P(None, 'head'), may hold values from -1 to 1
- key_weight: bfloat16 [5376, 2048], P(None, 'head'), may hold values from -1 to 1
- value_weight: bfloat16 [5376, 2048], P(None, 'head'), may hold values from -0.078125 to 0.078125
- output_grad: bfloat16 [4096, 4096], P('seq', 'head'), may hold values from -48 to 48
- segments: int32 [4096], replicated, may hold values from 0 to 3, never falling along the last dimension, each value on 1 to 2048 neighbouring positions
Outputs:
- token_grad: bfloat16 [4096, 5376], P('seq', 'head')
- query_weight_grad: bfloat16 [5376, 4096], P('seq', 'head')
- key_weight_grad: bfloat16 [5376, 2048], P('seq', 'head')
- value_weight_grad: bfloat16 [5376, 2048], P('seq', 'head')
Inputs may be any that keep to these rules, and one draw needn't show every extreme that they name: `segments`: segment numbers never fall along the tokens; a segment has at most 2048 tokens.
All inputs are finite; a program needn't handle non-finite values.
Results may differ from a plain program's by a relative error of at most 0.015.
The roundings to bfloat16 on the way count: a program that leaves them out, or rounds other values in their place, can miss the bound.
Values may be sent and summed in bfloat16 or wider, within the bound.
No kernel may reach another device: no remote copies, remote signals or barrier semaphores. Data moves between devices by JAX's collectives and lax.ppermute only.
A program may use at most 192 MiB of HBM per device.

v0:
```python
import jax
import jax.numpy as jnp
from jax import lax
from jax.sharding import Mesh, PartitionSpec as P

D = 5376
HEADS = 32
KV_HEADS = 16
HEAD_DIM = 128
WINDOW = 1024
HOPS = 2
SEQ = ("seq_hi", "core")
neg_large = -1e30


def passed_along(x, axis, by):
    count = lax.axis_size(axis)
    pairs = [(i, i + by) for i in range(count) if 0 <= i + by < count]
    return lax.ppermute(x, axis, pairs)


def contract_last(left, right):
    return lax.dot_general(
        left, right, (((1,), (1,)), ((), ())), preferred_element_type=jnp.float32
    )


def contract_first(left, right):
    return lax.dot_general(
        left, right, (((0,), (0,)), ((), ())), preferred_element_type=jnp.float32
    )


def attend(queries, key_value, grads, query_first, key_first, seg_query, seg_key):
    tok_rows = queries.shape[0]
    key_rows = key_value.shape[1]
    groups = HEADS // KV_HEADS
    kv_local = key_value.shape[2] // HEAD_DIM
    score_scale = (D / HEADS) ** (-0.5)
    query_four = queries.reshape(tok_rows, kv_local, groups, HEAD_DIM)
    grad_four = grads.reshape(tok_rows, kv_local, groups, HEAD_DIM)
    key_three = key_value[0].reshape(key_rows, kv_local, HEAD_DIM)
    value_three = key_value[1].reshape(key_rows, kv_local, HEAD_DIM)
    query_pos = query_first + jnp.arange(tok_rows, dtype=jnp.int32)
    key_pos = key_first + jnp.arange(key_rows, dtype=jnp.int32)
    spacing = query_pos[:, None] - key_pos[None, :]
    allowed = (
        (key_pos >= 0)[None, :]
        & (spacing >= 0)
        & (spacing < WINDOW)
        & (seg_query[:, None] == seg_key[None, :])
    )
    scores = (
        jnp.einsum("akgd,ckd->kgac", query_four, key_three, preferred_element_type=jnp.float32)
        * score_scale
    )
    masked = jnp.where(allowed, scores, neg_large)
    row_max = jnp.max(masked, axis=-1, keepdims=True)
    expo = jnp.where(allowed, jnp.exp(masked - row_max), 0.0)
    probs = expo / jnp.sum(expo, axis=-1, keepdims=True)
    dprobs = jnp.einsum(
        "akgd,ckd->kgac", grad_four, value_three, preferred_element_type=jnp.float32
    )
    center = jnp.sum(probs * dprobs, axis=-1, keepdims=True)
    dscores = (probs * (dprobs - center)).astype(jnp.bfloat16)
    probs_low = probs.astype(jnp.bfloat16)
    query_grad = (
        (
            jnp.einsum("kgac,ckd->akgd", dscores, key_three, preferred_element_type=jnp.float32)
            * score_scale
        )
        .reshape(tok_rows, -1)
        .astype(jnp.bfloat16)
    )
    key_grad = (
        jnp.einsum("kgac,akgd->ckd", dscores, query_four, preferred_element_type=jnp.float32)
        * score_scale
    ).reshape(key_rows, -1)
    value_grad = jnp.einsum(
        "kgac,akgd->ckd", probs_low, grad_four, preferred_element_type=jnp.float32
    ).reshape(key_rows, -1)
    return (query_grad, jnp.stack([key_grad, value_grad]))


def per_device(tokens, query_weight, key_weight, value_weight, output_grad, segments):
    tok_rows = tokens.shape[0]
    hop_count = HOPS
    margin = hop_count * tok_rows
    gathered = lax.all_gather(tokens, "head", axis=1, tiled=True)
    queries = jnp.dot(gathered, query_weight, preferred_element_type=jnp.float32).astype(
        jnp.bfloat16
    )
    keys_own = jnp.dot(gathered, key_weight, preferred_element_type=jnp.float32).astype(
        jnp.bfloat16
    )
    values_own = jnp.dot(gathered, value_weight, preferred_element_type=jnp.float32).astype(
        jnp.bfloat16
    )
    key_value = jnp.stack([keys_own, values_own])
    blocks = [key_value] * (hop_count + 1)
    for distance in range(1, hop_count + 1):
        blocks[hop_count - distance] = passed_along(key_value, SEQ, distance)
    keys_all = jnp.concatenate(blocks, axis=1)
    position = lax.axis_index(SEQ)
    query_first = position * tok_rows
    seg_query = lax.dynamic_slice_in_dim(segments, query_first, tok_rows, 0)
    seg_padded = jnp.concatenate([jnp.full((margin,), -1, jnp.int32), segments], axis=0)
    seg_key = lax.dynamic_slice_in_dim(seg_padded, query_first, (hop_count + 1) * tok_rows, 0)
    query_grad, kv_grad = attend(
        queries, keys_all, output_grad, query_first, query_first - margin, seg_query, seg_key
    )
    pieces = [
        kv_grad[:, block * tok_rows : (block + 1) * tok_rows] for block in range(hop_count + 1)
    ]
    carried = pieces[hop_count]
    for distance in range(1, hop_count + 1):
        back = passed_along(pieces[hop_count - distance].astype(jnp.bfloat16), SEQ, -distance)
        carried = carried + back.astype(jnp.float32)
    key_grad = carried[0].astype(jnp.bfloat16)
    value_grad = carried[1].astype(jnp.bfloat16)
    n_head = lax.axis_size("head")
    me = lax.axis_index("head")
    width = tokens.shape[1]

    def term(dest):
        start = dest * width
        part = contract_last(query_grad, lax.dynamic_slice_in_dim(query_weight, start, width, 0))
        part = part + contract_last(key_grad, lax.dynamic_slice_in_dim(key_weight, start, width, 0))
        part = part + contract_last(
            value_grad, lax.dynamic_slice_in_dim(value_weight, start, width, 0)
        )
        return part.astype(jnp.bfloat16)

    token_sum = None
    for shift in range(n_head - 1, 0, -1):
        sent = term((me + shift) % n_head)
        pairs = [(i, (i + shift) % n_head) for i in range(n_head)]
        got = lax.ppermute(sent, "head", pairs).astype(jnp.float32)
        token_sum = got if token_sum is None else token_sum + got
    own = term(me).astype(jnp.float32)
    token_grad = (own if token_sum is None else token_sum + own).astype(jnp.bfloat16)
    proj_grads = jnp.concatenate([query_grad, key_grad, value_grad], axis=1)
    weight_part = contract_first(proj_grads, gathered).astype(jnp.bfloat16)
    n_seq = lax.axis_size(SEQ)
    block = weight_part.shape[1] // n_seq

    def weight_block(dest):
        return lax.dynamic_slice_in_dim(weight_part, dest * block, block, 1)

    weight_sum = weight_block(position).astype(jnp.float32)
    for shift in range(n_seq - 1, 0, -1):
        sent = weight_block((position + shift) % n_seq)
        pairs = [(i, (i + shift) % n_seq) for i in range(n_seq)]
        weight_sum = weight_sum + lax.ppermute(sent, SEQ, pairs).astype(jnp.float32)
    summed = (weight_sum * (tok_rows * n_seq) ** (-0.5)).astype(jnp.bfloat16).T
    q_width = query_weight.shape[1]
    k_width = key_weight.shape[1]
    query_weight_grad = summed[:, :q_width]
    key_weight_grad = summed[:, q_width : q_width + k_width]
    value_weight_grad = summed[:, q_width + k_width :]
    return (token_grad, query_weight_grad, key_weight_grad, value_weight_grad)


def solution(mesh):
    n_seq = mesh.shape["seq"]
    n_head = mesh.shape["head"]
    view = Mesh(mesh.devices.reshape(n_seq // 2, 2, n_head), ("seq_hi", "core", "head"))
    in_specs = (
        P(SEQ, "head"),
        P(None, "head"),
        P(None, "head"),
        P(None, "head"),
        P(SEQ, "head"),
        P(),
    )
    out_specs = (P(SEQ, "head"),) * 4
    return jax.shard_map(
        per_device, mesh=view, in_specs=in_specs, out_specs=out_specs, check_vma=False
    )
```

profile of v0, /device:TPU:27, one launch (start us, length us, event | category | flops | bytes accessed | tf_op | source)
XLA Modules:
  0.0 638.8 jit_solution(9430814455776416603)
XLA Ops:
  8.0 2.3 copy.77
  10.5 2.6 fusion.16
  13.1 97.3 %all-gather.2.cloned.1.call-done = bf16[512,5376]{0,1:T(8,128)(2,1)} async-done(((bf16[512,1344]{0,1:T(8,128)(2,1)}), bf16[512,5376]{0,1:T(8,128)(2,1)}) %all-gather.2.cloned.1.call-update) | async-done | bytes 5505040 | tf_op jit(solution)/shard_map/all_gather | solution.py:89
  110.5 7.3 %fusion.53 = bf16[1,512,512]{2,1,0:T(8,128)(2,1)S(1)} fusion(bf16[512,5376]{0,1:T(8,128)(2,1)} %all-gather.2.cloned.1.call-done, bf16[5376,512]{1,0:T(8,128)(2,1)} %param.9), kind=kOutput, calls=%fused_computation.77 | convolution fusion | flops 2818834432 | bytes 11534336 | tf_op jit(solution)/shard_map/dot_general | solution.py:96
  117.9 5.7 fusion.52
  123.7 3.4 collective-permute-start.1
  127.2 3.1 collective-permute-start
  130.3 5.9 convolution_convert_fusion.1
  136.2 1.9 copy.76
  138.1 9.5 %collective-permute-done.1 = bf16[2,512,512]{2,1,0:T(8,128)(2,1)} collective-permute-done((bf16[2,512,512]{2,1,0:T(8,128)(2,1)S(1)}, bf16[2,512,512]{2,1,0:T(8,128)(2,1)}, u32[]{:S(2)}, u32[]{:S(2)}) %collective-permute-start.1) | collective-permute-done | bytes 1048608 | tf_op jit(solution)/shard_map/ppermute | solution.py:19
  147.5 14.7 %collective-permute-done = bf16[2,512,512]{2,1,0:T(8,128)(2,1)} collective-permute-done((bf16[2,512,512]{2,1,0:T(8,128)(2,1)S(1)}, bf16[2,512,512]{2,1,0:T(8,128)(2,1)}, u32[]{:S(2)}, u32[]{:S(2)}) %collective-permute-start) | collective-permute-done | bytes 1048608 | tf_op jit(solution)/shard_map/ppermute | solution.py:19
  162.2 1.7 maximum_maximum_fusion
  163.9 1.4 fusion.70
  166.7 4.0 reshape_squeeze.7
  170.8 13.6 %fusion.72 = (f32[4,2,512]{2,1,0:T(2,128)S(1)}, f32[4,2,512,1536]{2,3,1,0:T(8,128)}) fusion(pred[512,1536]{0,1:T(8,128)(4,1)S(1)} %copy-done.11, bf16[1536,4,128,1]{0,2,3,1:T(8,128)(2,1)S(1)} %copy.63, bf16[512,4,2,128]{0,3,2,1:T(8,128)(2,1)S(1)} %bitcast.81), kind=kOutput, calls=%fused_computation.110 | convolution fusion | flops 1642071552 | bytes 28590080 | tf_op jit(solution)/shard_map/sub | solution.py:59
  184.3 17.5 %fusion.1 = (f32[4,2,512]{2,1,0:T(2,128)S(1)}, f32[4,1536,512,2]{2,1,3,0:T(8,128)}) fusion(f32[4,2,512,1536]{2,3,1,0:T(8,128)} %get-tuple-element.28, f32[4,2,512]{2,1,0:T(2,128)S(1)} %get-tuple-element.27, bf16[512,4,2,128]{0,3,2,1:T(8,128)(2,1)} %bitcast.83, bf16[1536,4,128,1]{2,1,0,3:T(4,128)(2,1)} %bitcast.82), kind=kOutput, calls=%fused_computation.3 | convolution fusion | flops 1629483008 | bytes 52985856 | tf_op jit(solution)/shard_map/akgd,ckd->kgac/dot_general | solution.py:61
  201.9 17.0 %fusion.3 = bf16[4,2,512,1536]{2,3,1,0:T(8,128)(2,1)S(1)} fusion(f32[4,1536,512,2]{2,1,3,0:T(8,128)} %get-tuple-element.30, f32[4,2,512]{2,1,0:T(2,128)S(1)} %get-tuple-element.29, f32[4,2,512,1536]{2,3,1,0:T(8,128)} %get-tuple-element.28, f32[4,2,512]{2,1,0:T(2,128)S(1)} %get-tuple-element.27), kind=kLoop, calls=%fused_computation.5 | loop fusion | flops 25165824 | bytes 62947328 | tf_op jit(solution)/shard_map/convert_element_type | solution.py:65
  218.9 2.8 multiply_convert_fusion.1
  221.7 7.0 %fusion.13 = f32[4,128,1536]{2,1,0:T(8,128)} fusion(bf16[512,4,2,128]{0,3,2,1:T(8,128)(2,1)} %bitcast.80, bf16[4,2,512,1536]{2,3,1,0:T(8,128)(2,1)S(1)} %fusion.3), kind=kOutput, calls=%fused_computation.33 | convolution fusion | flops 1611399168 | bytes 16777216 | tf_op jit(solution)/shard_map/kgac,akgd->ckd/dot_general | solution.py:76
  228.7 11.0 %fusion.5 = f32[4,1536,128,1]{1,2,3,0:T(8,128)S(1)} fusion(bf16[512,4,2,128]{0,3,2,1:T(8,128)(2,1)} %bitcast.84, f32[4,2,512,1536]{2,3,1,0:T(8,128)} %get-tuple-element.28, f32[4,2,512]{2,1,0:T(2,128)S(1)} %get-tuple-element.27), kind=kOutput, calls=%fused_computation.10 | convolution fusion | flops 1623195648 | bytes 29376512 | tf_op jit(solution)/shard_map/kgac,akgd->ckd/dot_general | solution.py:79
  240.5 2.2 collective-permute-start.3
  242.7 1.9 collective-permute-start.2
  244.7 3.5 fusion.25
  248.2 3.2 fusion.27
  251.4 3.2 fusion.29
  254.7 13.9 %collective-permute-done.3 = bf16[2,512,512]{1,2,0:T(8,128)(2,1)S(1)} collective-permute-done((bf16[2,512,512]{1,2,0:T(8,128)(2,1)S(1)}, bf16[2,512,512]{1,2,0:T(8,128)(2,1)S(1)}, u32[]{:S(2)}, u32[]{:S(2)}) %collective-permute-start.3) | collective-permute-done | bytes 1048608 | tf_op jit(solution)/shard_map/ppermute | solution.py:19
  268.5 3.7 collective-permute-done.2
  273.7 2.2 convolution_add_fusion.3
  275.9 3.3 fusion.19
  279.3 2.9 collective-permute-start.6
  282.1 19.3 %convolution_convert_fusion = bf16[2048,5376]{0,1:T(8,128)(2,1)} fusion(bf16[512,5376]{0,1:T(8,128)(2,1)} %all-gather.2.cloned.1.call-done, bf16[512,512]{0,1:T(8,128)(2,1)} %get-tuple-element.26, bf16[512,512]{0,1:T(8,128)(2,1)} %get-tuple-element.25, bf16[512,1024]{0,1:T(8,128)(2,1)S(1)} %bitcast.88), kind=kOutput, calls=%fused_computation.8 | convolution fusion | flops 11291590656 | bytes 29622272 | tf_op jit(solution)/shard_map/dot_general | solution.py:29
  301.4 12.4 %constant_dynamic-slice_fusion.6 = (bf16[2048,672]{0,1:T(8,128)(2,1)}, bf16[2048,672]{0,1:T(8,128)(2,1)S(1)}, bf16[2048,672]{0,1:T(8,128)(2,1)S(1)}, bf16[2048,6...) fusion(bf16[2048,5376]{0,1:T(8,128)(2,1)} %convolution_convert_fusion, ...), kind=kLoop, calls=%fused_computation.89 | loop fusion | bytes 38535196 | tf_op jit(solution)/shard_map/dynamic_slice | solution.py:148
  314.0 1.2 collective-permute-start.12
  315.1 2.2 convolution_add_fusion.5
  317.4 2.4 fusion.18
  319.9 2.2 convolution_add_fusion.7
  322.1 2.2 fusion.17
  324.9 85.2 %collective-permute-done.5 = bf16[512,1344]{0,1:T(8,128)(2,1)S(1)} collective-permute-done((bf16[512,1344]{0,1:T(8,128)(2,1)S(1)}, bf16[512,1344]{0,1:T(8,128)(2,1)S(1)}, u32[]{:S(2)}, u32[]{:S(2)}) %collective-permute-start.5) | collective-permute-done | bytes 1376288 | tf_op jit(solution)/shard_map/ppermute | solution.py:138
  411.1 2.4 collective-permute-start.8
  413.5 16.9 %collective-permute-done.12 = bf16[2048,672]{0,1:T(8,128)(2,1)} collective-permute-done((bf16[2048,672]{0,1:T(8,128)(2,1)S(1)}, bf16[2048,672]{0,1:T(8,128)(2,1)}, u32[]{:S(2)}, u32[]{:S(2)}) %collective-permute-start.12) | collective-permute-done | bytes 2752544 | tf_op jit(solution)/shard_map/ppermute | solution.py:154
  430.6 3.4 fusion.23
  434.0 2.4 convolution_add_fusion.1
  436.5 3.7 add_convert_fusion
  440.2 149.0 %collective-permute-done.10 = bf16[2048,672]{0,1:T(8,128)(2,1)} collective-permute-done((bf16[2048,672]{0,1:T(8,128)(2,1)}, bf16[2048,672]{0,1:T(8,128)(2,1)}, u32[]{:S(2)}, u32[]{:S(2)}) %collective-permute-start.10) | collective-permute-done | bytes 2752544 | tf_op jit(solution)/shard_map/ppermute | solution.py:154
  589.2 30.1 %collective-permute-done.9 = bf16[2048,672]{0,1:T(8,128)(2,1)} collective-permute-done((bf16[2048,672]{0,1:T(8,128)(2,1)}, bf16[2048,672]{0,1:T(8,128)(2,1)}, u32[]{:S(2)}, u32[]{:S(2)}) %collective-permute-start.9) | collective-permute-done | bytes 2752544 | tf_op jit(solution)/shard_map/ppermute | solution.py:154
  619.3 9.9 %fusion.22 = bf16[672,2048]{1,0:T(8,128)(2,1)S(1)} fusion(bf16[2048,672]{0,1:T(8,128)(2,1)} %collective-permute-done.13, bf16[2048,672]{0,1:T(8,128)(2,1)} %collective-permute-done.12, bf16[2048,672]{0,1:T(8,128)(2,1)} %collective-permute-done.11, bf16[2048,672]{0,1:T(8,128)(2,1)} %collective-permute-done.10, bf16[2048,672]{0,1:T(8,128)(2,1)} %collective-permute-done.9, ...), kind=kLoop, calls=%fused_computation.43 | loop fusion | flops 23396352 | bytes 24772612 | tf_op jit(solution)/shard_map/transpose | solution.py:155
  629.3 1.2 slice.52
  630.5 1.2 fusion.71
  (68 shorter events, 6.7 us)
Async XLA Ops:
  7.2 3.2 copy-start.12
  7.2 103.3 %all-gather.2.cloned.1.call-start = ((), (), s32[]{:S(2)}) async-start(), calls=%async_computation | async-start | bytes 6881280 | tf_op jit(solution)/shard_map/all_gather | solution.py:89
  110.5 7.4 %copy-start.13 = (bf16[512,5376]{0,1:T(8,128)(2,1)S(1)}, bf16[512,5376]{0,1:T(8,128)(2,1)}, u32[]{:S(2)}) copy-start(bf16[512,5376]{0,1:T(8,128)(2,1)} %all-gather.2.cloned.1.call-done) | copy-start | bytes 16515076
  110.5 19.8 %slice-start = ((s8[11010048]{0:T(1024)(128)(4,1)}), s8[4194304]{0:T(1024)(128)(4,1)S(1)}, s32[]{:S(2)}) async-start(s8[11010048]{0:T(1024)(128)(4,1)} %bitcast.90), calls=%async_computation.1 | async-start | bytes 8388608
  110.5 19.8 %slice-start.1 = ((s8[11010048]{0:T(1024)(128)(4,1)}), s8[4194304]{0:T(1024)(128)(4,1)S(1)}, s32[]{:S(2)}) async-start(s8[11010048]{0:T(1024)(128)(4,1)} %bitcast.90), calls=%async_computation.2 | async-start | bytes 8388608
  117.9 12.5 %slice-start.2 = ((s8[11010048]{0:T(1024)(128)(4,1)}), s8[2621440]{0:T(1024)(128)(4,1)S(1)}, s32[]{:S(2)}) async-start(s8[11010048]{0:T(1024)(128)(4,1)} %bitcast.90), calls=%async_computation.3 | async-start | bytes 5242880
  123.7 23.8 %collective-permute-start.1 = (bf16[2,512,512]{2,1,0:T(8,128)(2,1)S(1)}, bf16[2,512,512]{2,1,0:T(8,128)(2,1)}, u32[]{:S(2)}, u32[]{:S(2)}) collective-permute-start(bf16[2,512,512]{2,1,0:T(8,128)(2,1)S(1)} %pad_maximum_fusion.1), channel_id=1, source_target_pairs={{0,4},{4,8},{8,12},{12,16},{16,20},{20,24},{24,28},{1,5},{5,9},{9,... | collective-permute-start | bytes 3145736 | tf_op jit(solution)/shard_map/ppermute | solution.py:19
  127.2 35.0 %collective-permute-start = (bf16[2,512,512]{2,1,0:T(8,128)(2,1)S(1)}, bf16[2,512,512]{2,1,0:T(8,128)(2,1)}, u32[]{:S(2)}, u32[]{:S(2)}) collective-permute-start(bf16[2,512,512]{2,1,0:T(8,128)(2,1)S(1)} %pad_maximum_fusion.1), channel_id=1, source_target_pairs={{0,8},{4,12},{8,16},{12,20},{16,24},{20,28},{1,9},{5,13},{9,17},{1... | collective-permute-start | bytes 3145736 | tf_op jit(solution)/shard_map/ppermute | solution.py:19
  166.7 17.7 %copy-start.1 = (bf16[1536,4,128,1]{0,2,3,1:T(8,128)(2,1)}, bf16[1536,4,128,1]{0,2,3,1:T(8,128)(2,1)S(1)}, u32[]{:S(2)}) copy-start(bf16[1536,4,128,1]{0,2,3,1:T(8,128)(2,1)S(1)} %copy.63) | copy-start | bytes 4718596
  166.7 4.1 copy-start.3
  166.7 4.1 copy-start.11
  201.9 17.0 %copy-start.2 = (bf16[1536,4,128,1]{0,2,3,1:T(8,128)(2,1)S(1)}, bf16[1536,4,128,1]{0,2,3,1:T(8,128)(2,1)}, u32[]{:S(2)}) copy-start(bf16[1536,4,128,1]{0,2,3,1:T(8,128)(2,1)} %copy-done.1) | copy-start | bytes 4718596
  228.7 11.0 %copy-start = (f32[4,128,1536]{2,1,0:T(8,128)S(1)}, f32[4,128,1536]{2,1,0:T(8,128)}, u32[]{:S(2)}) copy-start(f32[4,128,1536]{2,1,0:T(8,128)} %fusion.13) | copy-start | bytes 9437188
  239.7 8.5 %slice-start.3 = ((s8[11010048]{0:T(1024)(128)(4,1)}), s8[2621440]{0:T(1024)(128)(4,1)S(1)}, s32[]{:S(2)}) async-start(s8[11010048]{0:T(1024)(128)(4,1)} %bitcast.92), calls=%async_computation.4 | async-start | bytes 5242880
  239.7 8.5 %slice-start.4 = ((s8[11010048]{0:T(1024)(128)(4,1)}), s8[4194304]{0:T(1024)(128)(4,1)S(1)}, s32[]{:S(2)}) async-start(s8[11010048]{0:T(1024)(128)(4,1)} %bitcast.92), calls=%async_computation.5 | async-start | bytes 8388608
  240.3 4.4 copy-start.10
  240.5 28.0 %collective-permute-start.3 = (bf16[2,512,512]{1,2,0:T(8,128)(2,1)S(1)}, bf16[2,512,512]{1,2,0:T(8,128)(2,1)S(1)}, u32[]{:S(2)}, u32[]{:S(2)}) collective-permute-start(bf16[2,512,512]{1,2,0:T(8,128)(2,1)S(1)} %get-tuple-element.20), channel_id=1, source_target_pairs={{8,0},{12,4},{16,8},{20,12},{24,16},{28,20},{9,1},{13,5},{17,9},{2... | collective-permute-start | bytes 3145736 | tf_op jit(solution)/shard_map/ppermute | solution.py:19
  242.7 29.5 %collective-permute-start.2 = (bf16[2,512,512]{1,2,0:T(8,128)(2,1)S(1)}, bf16[2,512,512]{1,2,0:T(8,128)(2,1)S(1)}, u32[]{:S(2)}, u32[]{:S(2)}) collective-permute-start(bf16[2,512,512]{1,2,0:T(8,128)(2,1)S(1)} %get-tuple-element.19), channel_id=1, source_target_pairs={{4,0},{8,4},{12,8},{16,12},{20,16},{24,20},{28,24},{5,1},{9,5},{13... | collective-permute-start | bytes 3145736 | tf_op jit(solution)/shard_map/ppermute | solution.py:19
  244.7 3.6 slice-start.5
  279.3 45.3 %collective-permute-start.6 = (bf16[512,1344]{0,1:T(8,128)(2,1)}, bf16[512,1344]{0,1:T(8,128)(2,1)S(1)}, u32[]{:S(2)}, u32[]{:S(2)}) collective-permute-start(bf16[512,1344]{0,1:T(8,128)(2,1)} %fusion.19), channel_id=1, source_target_pairs={{0,1},{1,2},{2,3},{3,0},{4,5},{5,6},{6,7},{7,4},{8,9},{9,10},{10,1... | collective-permute-start | bytes 4128776 | tf_op jit(solution)/shard_map/ppermute | solution.py:138
  301.4 13.7 %copy-start.5 = (f32[512,1344]{0,1:T(8,128)S(1)}, f32[512,1344]{0,1:T(8,128)}, u32[]{:S(2)}) copy-start(f32[512,1344]{0,1:T(8,128)} %fusion.27) | copy-start | bytes 8257540
  313.9 97.3 %collective-permute-start.13 = (bf16[2048,672]{0,1:T(8,128)(2,1)S(1)}, bf16[2048,672]{0,1:T(8,128)(2,1)}, u32[]{:S(2)}, u32[]{:S(2)}) collective-permute-start(bf16[2048,672]{0,1:T(8,128)(2,1)S(1)} %get-tuple-element.13), channel_id=1, source_target_pairs={{0,4},{4,8},{8,12},{12,16},{16,20},{20,24},{24,28},{28,0},{1,5},{5... | collective-permute-start | bytes 8257544 | tf_op jit(solution)/shard_map/ppermute | solution.py:154
  314.0 116.4 %collective-permute-start.12 = (bf16[2048,672]{0,1:T(8,128)(2,1)S(1)}, bf16[2048,672]{0,1:T(8,128)(2,1)}, u32[]{:S(2)}, u32[]{:S(2)}) collective-permute-start(bf16[2048,672]{0,1:T(8,128)(2,1)S(1)} %get-tuple-element.14), channel_id=1, source_target_pairs={{0,8},{4,12},{8,16},{12,20},{16,24},{20,28},{24,0},{28,4},{1,9},{5... | collective-permute-start | bytes 8257544 | tf_op jit(solution)/shard_map/ppermute | solution.py:154
  317.4 2.5 copy-start.4
  319.8 90.4 %collective-permute-start.5 = (bf16[512,1344]{0,1:T(8,128)(2,1)S(1)}, bf16[512,1344]{0,1:T(8,128)(2,1)S(1)}, u32[]{:S(2)}, u32[]{:S(2)}) collective-permute-start(bf16[512,1344]{0,1:T(8,128)(2,1)S(1)} %fusion.18), channel_id=1, source_target_pairs={{0,2},{1,3},{2,0},{3,1},{4,6},{5,7},{6,4},{7,5},{8,10},{9,11},{10,... | collective-permute-start | bytes 4128776 | tf_op jit(solution)/shard_map/ppermute | solution.py:138
  324.3 85.8 %collective-permute-start.4 = (bf16[512,1344]{0,1:T(8,128)(2,1)S(1)}, bf16[512,1344]{0,1:T(8,128)(2,1)S(1)}, u32[]{:S(2)}, u32[]{:S(2)}) collective-permute-start(bf16[512,1344]{0,1:T(8,128)(2,1)S(1)} %fusion.17), channel_id=1, source_target_pairs={{0,3},{1,0},{2,1},{3,2},{4,7},{5,4},{6,5},{7,6},{8,11},{9,8},{10,9... | collective-permute-start | bytes 4128776 | tf_op jit(solution)/shard_map/ppermute | solution.py:138
  324.6 115.6 %collective-permute-start.11 = (bf16[2048,672]{0,1:T(8,128)(2,1)}, bf16[2048,672]{0,1:T(8,128)(2,1)}, u32[]{:S(2)}, u32[]{:S(2)}) collective-permute-start(bf16[2048,672]{0,1:T(8,128)(2,1)} %get-tuple-element.15), channel_id=1, source_target_pairs={{0,12},{4,16},{8,20},{12,24},{16,28},{20,0},{24,4},{28,8},{1,13},{... | collective-permute-start | bytes 8257544 | tf_op jit(solution)/shard_map/ppermute | solution.py:154
  410.1 20.2 %copy-start.6 = (bf16[512,1344]{0,1:T(8,128)(2,1)}, bf16[512,1344]{0,1:T(8,128)(2,1)S(1)}, u32[]{:S(2)}) copy-start(bf16[512,1344]{0,1:T(8,128)(2,1)S(1)} %collective-permute-done.5) | copy-start | bytes 4128772
  410.1 179.0 %collective-permute-start.10 = (bf16[2048,672]{0,1:T(8,128)(2,1)}, bf16[2048,672]{0,1:T(8,128)(2,1)}, u32[]{:S(2)}, u32[]{:S(2)}) collective-permute-start(bf16[2048,672]{0,1:T(8,128)(2,1)} %get-tuple-element.16), channel_id=1, source_target_pairs={{0,16},{4,20},{8,24},{12,28},{16,0},{20,4},{24,8},{28,12},{1,17},{... | collective-permute-start | bytes 8257544 | tf_op jit(solution)/shard_map/ppermute | solution.py:154
  410.2 20.2 %copy-start.8 = (bf16[512,1344]{0,1:T(8,128)(2,1)}, bf16[512,1344]{0,1:T(8,128)(2,1)S(1)}, u32[]{:S(2)}) copy-start(bf16[512,1344]{0,1:T(8,128)(2,1)S(1)} %collective-permute-done.4) | copy-start | bytes 4128772
  410.2 209.2 %collective-permute-start.9 = (bf16[2048,672]{0,1:T(8,128)(2,1)}, bf16[2048,672]{0,1:T(8,128)(2,1)}, u32[]{:S(2)}, u32[]{:S(2)}) collective-permute-start(bf16[2048,672]{0,1:T(8,128)(2,1)} %get-tuple-element.17), channel_id=1, source_target_pairs={{0,20},{4,24},{8,28},{12,0},{16,4},{20,8},{24,12},{28,16},{1,21},{... | collective-permute-start | bytes 8257544 | tf_op jit(solution)/shard_map/ppermute | solution.py:154
  411.1 208.2 %collective-permute-start.8 = (bf16[2048,672]{0,1:T(8,128)(2,1)}, bf16[2048,672]{0,1:T(8,128)(2,1)}, u32[]{:S(2)}, u32[]{:S(2)}) collective-permute-start(bf16[2048,672]{0,1:T(8,128)(2,1)} %get-tuple-element.18), channel_id=1, source_target_pairs={{0,24},{4,28},{8,0},{12,4},{16,8},{20,12},{24,16},{28,20},{1,25},{... | collective-permute-start | bytes 8257544 | tf_op jit(solution)/shard_map/ppermute | solution.py:154
  430.4 188.9 %collective-permute-start.7 = (bf16[2048,672]{0,1:T(8,128)(2,1)}, bf16[2048,672]{0,1:T(8,128)(2,1)}, u32[]{:S(2)}, u32[]{:S(2)}) collective-permute-start(bf16[2048,672]{0,1:T(8,128)(2,1)} %get-tuple-element.12), channel_id=1, source_target_pairs={{0,28},{4,0},{8,4},{12,8},{16,12},{20,16},{24,20},{28,24},{1,29},{... | collective-permute-start | bytes 8257544 | tf_op jit(solution)/shard_map/ppermute | solution.py:154
  434.0 2.4 copy-start.7
  434.0 2.4 copy-start.9
Sparse Core Ops, SparseCore 0:
  9.6 100.8 all-gather.1
where the time goes:
time: 646 us; the launch traced here: 639 us
  waiting for transfers between devices  421 us (65%)
  matrix products  124 us (19%)
  other arithmetic  32.4 us (5%)
  local copies, waits for them, and re-layouts  27.2 us (4%)
  starting transfers between devices  19 us (3%)
  between operations  14.9 us (2%)
    ppermute x7, waiting for transfers between devices, per_device(): weight_sum = weight_sum + lax.ppermute(sent, SEQ, pairs).astype(jnp.float32)  196 us
    all_gather x1, waiting for transfers between devices, per_device(): gathered = lax.all_gather(tokens, 'head', axis=1, tiled=True)  97.3 us
    ppermute x3, waiting for transfers between devices, per_device(): got = lax.ppermute(sent, 'head', pairs).astype(jnp.float32)  85.2 us
    ppermute x4, waiting for transfers between devices, passed_along(): return lax.ppermute(x, axis, pairs)  41.7 us
    dot_general x12, matrix products, contract_last(): lax.dot_general(left, right, (((1,), (1,)), ((), ())), preferred_element_...  34 us
    dot_general x1, matrix products, contract_first(): lax.dot_general(left, right, (((0,), (0,)), ((), ())), preferred_element_...  19.3 us
    dot_general x1, matrix products, attend(): jnp.einsum('akgd,ckd->kgac', grad_four, value_three, preferred_element_ty...  17.5 us
    convert_element_type x1, other arithmetic, attend(): dscores = (probs * (dprobs - center)).astype(jnp.bfloat16)  17 us
  transfers between devices with their start and end apart: 15, of which 9 were waited for; matrix products, arithmetic and copies ran while one was open for 11% of the time, Pallas kernels for 0%

commit v1 on v0

--- a/solution.py
+++ b/solution.py
@@ -11,6 +11,24 @@
 HOPS = 2
 SEQ = ("seq_hi", "core")
 neg_large = -1e30
+
+
+def ring_gather(array, axis, dim):
+    ways, here, step = (lax.axis_size(axis), lax.axis_index(axis), array.shape[dim])
+    shape = [n * ways if d == dim else n for d, n in enumerate(array.shape)]
+    full = lax.dynamic_update_slice_in_dim(
+        jnp.zeros(shape, array.dtype), array, here * step, axis=dim
+    )
+    going_up = going_down = array
+    for far in range(1, ways // 2 + 1):
+        going_up = lax.ppermute(going_up, axis, [(d, (d + 1) % ways) for d in range(ways)])
+        full = lax.dynamic_update_slice_in_dim(full, going_up, (here - far) % ways * step, axis=dim)
+        if 2 * far < ways:
+            going_down = lax.ppermute(going_down, axis, [(d, (d - 1) % ways) for d in range(ways)])
+            full = lax.dynamic_update_slice_in_dim(
+                full, going_down, (here + far) % ways * step, axis=dim
+            )
+    return full
 
 
 def passed_along(x, axis, by):
@@ -86,7 +104,7 @@
     tok_rows = tokens.shape[0]
     hop_count = HOPS
     margin = hop_count * tok_rows
-    gathered = lax.all_gather(tokens, "head", axis=1, tiled=True)
+    gathered = ring_gather(tokens, "head", 1)
     queries = jnp.dot(gathered, query_weight, preferred_element_type=jnp.float32).astype(
         jnp.bfloat16
     )

time: 646 us -> 616 us (0.954)
  waiting for transfers between devices: 421 us -> 400 us
  between operations: 14.9 us -> 1.68 us
  matrix products: 124 us -> 117 us
    all_gather x1 -> x0, waiting for transfers between devices: 97.3 us -> none  [per_device(): gathered = lax.all_gather(tokens, 'head', axis=1, tiled=True)]
    ppermute x0 -> x3, waiting for transfers between devices: none -> 76.1 us  [the longest x2 55.9 us: ring_gather(): lax.ppermute(going_up, axis, [(d, (d + 1) % ways) for d in range(ways)])]
  transfers between devices with their start and end apart: 15 -> 17, of which waited for: 9 -> 11; matrix products, arithmetic and copies ran while one was open for 11% -> 13% of each run, Pallas kernels for 0% -> 0%
where the time goes in v1:
time: 616 us; the launch traced here: 608 us
  waiting for transfers between devices  400 us (65%)
  matrix products  117 us (19%)
  other arithmetic  33.1 us (5%)
  local copies, waits for them, and re-layouts  32.2 us (5%)
  starting transfers between devices  23.9 us (4%)
    ppermute x7, waiting for transfers between devices, per_device(): weight_sum = weight_sum + lax.ppermute(sent, SEQ, pairs).astype(jnp.float32)  196 us
    ppermute x3, waiting for transfers between devices, per_device(): got = lax.ppermute(sent, 'head', pairs).astype(jnp.float32)  86.3 us
    ppermute x2, waiting for transfers between devices, ring_gather(): lax.ppermute(going_up, axis, [(d, (d + 1) % ways) for d in range(ways)])  55.9 us
    ppermute x4, waiting for transfers between devices, passed_along(): return lax.ppermute(x, axis, pairs)  42 us
    dot_general x12, matrix products, contract_last(): lax.dot_general(left, right, (((1,), (1,)), ((), ())), preferred_element_...  34 us
    ppermute x1, waiting for transfers between devices, ring_gather(): lax.ppermute(going_down, axis, [(d, (d - 1) % ways) for d in range(ways)])  20.2 us
    dot_general x1, matrix products, contract_first(): lax.dot_general(left, right, (((0,), (0,)), ((), ())), preferred_element_...  19.3 us
    dot_general x1, matrix products, attend(): jnp.einsum('akgd,ckd->kgac', grad_four, value_three, preferred_element_ty...  17.5 us
  transfers between devices with their start and end apart: 17, of which 11 were waited for; matrix products, arithmetic and copies ran while one was open for 13% of the time, Pallas kernels for 0%

profile of v1, /device:TPU:27, one launch (start us, length us, event | category | flops | bytes accessed | tf_op | source)
XLA Modules:
  0.0 608.4 jit_solution(9467733832261084733)
XLA Ops:
  2.9 29.2 %collective-permute-done = bf16[512,1344]{0,1:T(8,128)(2,1)S(1)} collective-permute-done((bf16[512,1344]{0,1:T(8,128)(2,1)}, bf16[512,1344]{0,1:T(8,128)(2,1)S(1)}, u32[]{:S(2)}, u32[]{:S(2)}) %collective-permute-start) | collective-permute-done | bytes 1376288 | tf_op jit(solution)/shard_map/ppermute | solution.py:24
  32.2 1.7 collective-permute-start.2
  34.6 2.3 copy.77
  38.4 2.7 fusion.16
  41.2 20.2 %collective-permute-done.1 = bf16[512,1344]{0,1:T(8,128)(2,1)} collective-permute-done((bf16[512,1344]{0,1:T(8,128)(2,1)}, bf16[512,1344]{0,1:T(8,128)(2,1)}, u32[]{:S(2)}, u32[]{:S(2)}) %collective-permute-start.1) | collective-permute-done | bytes 1376288 | tf_op jit(solution)/shard_map/ppermute | solution.py:27
  62.8 26.7 %collective-permute-done.2 = bf16[512,1344]{0,1:T(8,128)(2,1)} collective-permute-done((bf16[512,1344]{0,1:T(8,128)(2,1)S(1)}, bf16[512,1344]{0,1:T(8,128)(2,1)}, u32[]{:S(2)}, u32[]{:S(2)}) %collective-permute-start.2) | collective-permute-done | bytes 1376288 | tf_op jit(solution)/shard_map/ppermute | solution.py:24
  89.5 1.6 constant_dynamic-update-slice_fusion
  91.2 3.0 fusion.53
  94.3 3.0 fusion.52
  97.4 6.1 collective-permute-start.4
  103.5 3.1 collective-permute-start.3
  106.7 5.9 convolution_convert_fusion.1
  112.6 1.5 copy.76
  114.1 9.8 %collective-permute-done.4 = bf16[2,512,512]{2,1,0:T(8,128)(2,1)} collective-permute-done((bf16[2,512,512]{2,1,0:T(8,128)(2,1)S(1)}, bf16[2,512,512]{2,1,0:T(8,128)(2,1)}, u32[]{:S(2)}, u32[]{:S(2)}) %collective-permute-start.4) | collective-permute-done | bytes 1048608 | tf_op jit(solution)/shard_map/ppermute | solution.py:37
  123.9 14.6 %collective-permute-done.3 = bf16[2,512,512]{2,1,0:T(8,128)(2,1)} collective-permute-done((bf16[2,512,512]{2,1,0:T(8,128)(2,1)S(1)}, bf16[2,512,512]{2,1,0:T(8,128)(2,1)}, u32[]{:S(2)}, u32[]{:S(2)}) %collective-permute-start.3) | collective-permute-done | bytes 1048608 | tf_op jit(solution)/shard_map/ppermute | solution.py:37
  138.5 1.7 maximum_maximum_fusion
  143.0 4.0 reshape_squeeze.7
  147.1 13.6 %fusion.72 = (f32[4,2,512]{2,1,0:T(2,128)S(1)}, f32[4,2,512,1536]{2,3,1,0:T(8,128)}) fusion(pred[512,1536]{0,1:T(8,128)(4,1)S(1)} %copy-done.13, bf16[1536,4,128,1]{0,2,3,1:T(8,128)(2,1)S(1)} %copy.63, bf16[512,4,2,128]{0,3,2,1:T(8,128)(2,1)S(1)} %bitcast.85), kind=kOutput, calls=%fused_computation.114 | convolution fusion | flops 1642071552 | bytes 28590080 | tf_op jit(solution)/shard_map/sub | solution.py:77
  160.6 17.5 %fusion.1 = (f32[4,2,512]{2,1,0:T(2,128)S(1)}, f32[4,1536,512,2]{2,1,3,0:T(8,128)}) fusion(f32[4,2,512,1536]{2,3,1,0:T(8,128)} %get-tuple-element.28, f32[4,2,512]{2,1,0:T(2,128)S(1)} %get-tuple-element.27, bf16[512,4,2,128]{0,3,2,1:T(8,128)(2,1)} %bitcast.87, bf16[1536,4,128,1]{2,1,0,3:T(4,128)(2,1)} %bitcast.86), kind=kOutput, calls=%fused_computation.3 | convolution fusion | flops 1629483008 | bytes 52985856 | tf_op jit(solution)/shard_map/akgd,ckd->kgac/dot_general | solution.py:79
  178.1 17.0 %fusion.3 = bf16[4,2,512,1536]{2,3,1,0:T(8,128)(2,1)S(1)} fusion(f32[4,1536,512,2]{2,1,3,0:T(8,128)} %get-tuple-element.30, f32[4,2,512]{2,1,0:T(2,128)S(1)} %get-tuple-element.29, f32[4,2,512,1536]{2,3,1,0:T(8,128)} %get-tuple-element.28, f32[4,2,512]{2,1,0:T(2,128)S(1)} %get-tuple-element.27), kind=kLoop, calls=%fused_computation.5 | loop fusion | flops 25165824 | bytes 62947328 | tf_op jit(solution)/shard_map/convert_element_type | solution.py:83
  195.1 2.9 multiply_convert_fusion.1
  197.9 7.0 %fusion.13 = f32[4,128,1536]{2,1,0:T(8,128)} fusion(bf16[512,4,2,128]{0,3,2,1:T(8,128)(2,1)} %bitcast.84, bf16[4,2,512,1536]{2,3,1,0:T(8,128)(2,1)S(1)} %fusion.3), kind=kOutput, calls=%fused_computation.33 | convolution fusion | flops 1611399168 | bytes 16777216 | tf_op jit(solution)/shard_map/kgac,akgd->ckd/dot_general | solution.py:94
  204.9 11.0 %fusion.5 = f32[4,1536,128,1]{1,2,3,0:T(8,128)S(1)} fusion(bf16[512,4,2,128]{0,3,2,1:T(8,128)(2,1)} %bitcast.88, f32[4,2,512,1536]{2,3,1,0:T(8,128)} %get-tuple-element.28, f32[4,2,512]{2,1,0:T(2,128)S(1)} %get-tuple-element.27), kind=kOutput, calls=%fused_computation.10 | convolution fusion | flops 1623195648 | bytes 29376512 | tf_op jit(solution)/shard_map/kgac,akgd->ckd/dot_general | solution.py:97
  216.8 2.2 collective-permute-start.6
  219.0 1.9 collective-permute-start.5
  220.9 3.5 fusion.25
  224.5 3.2 fusion.27
  227.7 3.2 fusion.29
  230.9 13.9 %collective-permute-done.6 = bf16[2,512,512]{1,2,0:T(8,128)(2,1)S(1)} collective-permute-done((bf16[2,512,512]{1,2,0:T(8,128)(2,1)S(1)}, bf16[2,512,512]{1,2,0:T(8,128)(2,1)S(1)}, u32[]{:S(2)}, u32[]{:S(2)}) %collective-permute-start.6) | collective-permute-done | bytes 1048608 | tf_op jit(solution)/shard_map/ppermute | solution.py:37
  244.8 3.6 collective-permute-done.5
  249.9 2.2 convolution_add_fusion.3
  252.2 3.3 fusion.19
  255.5 1.9 collective-permute-start.9
  257.3 19.3 %convolution_convert_fusion = bf16[2048,5376]{0,1:T(8,128)(2,1)} fusion(bf16[512,5376]{0,1:T(8,128)(2,1)} %copy-done.3, bf16[512,512]{0,1:T(8,128)(2,1)} %get-tuple-element.26, bf16[512,512]{0,1:T(8,128)(2,1)} %get-tuple-element.25, bf16[512,1024]{0,1:T(8,128)(2,1)S(1)} %bitcast.92), kind=kOutput, calls=%fused_computation.8 | convolution fusion | flops 11291590656 | bytes 29622272 | tf_op jit(solution)/shard_map/dot_general | solution.py:47
  276.7 12.4 %constant_dynamic-slice_fusion.6 = (bf16[2048,672]{0,1:T(8,128)(2,1)}, bf16[2048,672]{0,1:T(8,128)(2,1)S(1)}, bf16[2048,672]{0,1:T(8,128)(2,1)S(1)}, bf16[2048,6...) fusion(bf16[2048,5376]{0,1:T(8,128)(2,1)} %convolution_convert_fusion, ...), kind=kLoop, calls=%fused_computation.89 | loop fusion | bytes 38535196 | tf_op jit(solution)/shard_map/dynamic_slice | solution.py:166
  290.4 2.2 convolution_add_fusion.5
  292.7 2.4 fusion.18
  295.1 2.2 convolution_add_fusion.7
  297.4 2.2 fusion.17
  300.2 86.3 %collective-permute-done.8 = bf16[512,1344]{0,1:T(8,128)(2,1)S(1)} collective-permute-done((bf16[512,1344]{0,1:T(8,128)(2,1)S(1)}, bf16[512,1344]{0,1:T(8,128)(2,1)S(1)}, u32[]{:S(2)}, u32[]{:S(2)}) %collective-permute-start.8) | collective-permute-done | bytes 1376288 | tf_op jit(solution)/shard_map/ppermute | solution.py:156
  387.4 2.4 collective-permute-start.11
  389.8 15.8 %collective-permute-done.15 = bf16[2048,672]{0,1:T(8,128)(2,1)} collective-permute-done((bf16[2048,672]{0,1:T(8,128)(2,1)S(1)}, bf16[2048,672]{0,1:T(8,128)(2,1)}, u32[]{:S(2)}, u32[]{:S(2)}) %collective-permute-start.15) | collective-permute-done | bytes 2752544 | tf_op jit(solution)/shard_map/ppermute | solution.py:172
  405.9 3.4 fusion.23
  409.3 2.4 convolution_add_fusion.1
  411.7 3.7 add_convert_fusion
  415.4 150.1 %collective-permute-done.13 = bf16[2048,672]{0,1:T(8,128)(2,1)} collective-permute-done((bf16[2048,672]{0,1:T(8,128)(2,1)}, bf16[2048,672]{0,1:T(8,128)(2,1)}, u32[]{:S(2)}, u32[]{:S(2)}) %collective-permute-start.13) | collective-permute-done | bytes 2752544 | tf_op jit(solution)/shard_map/ppermute | solution.py:172
  565.5 30.1 %collective-permute-done.12 = bf16[2048,672]{0,1:T(8,128)(2,1)} collective-permute-done((bf16[2048,672]{0,1:T(8,128)(2,1)}, bf16[2048,672]{0,1:T(8,128)(2,1)}, u32[]{:S(2)}, u32[]{:S(2)}) %collective-permute-start.12) | collective-permute-done | bytes 2752544 | tf_op jit(solution)/shard_map/ppermute | solution.py:172
  595.6 9.9 %fusion.22 = bf16[672,2048]{1,0:T(8,128)(2,1)S(1)} fusion(bf16[2048,672]{0,1:T(8,128)(2,1)} %collective-permute-done.16, bf16[2048,672]{0,1:T(8,128)(2,1)} %collective-permute-done.15, bf16[2048,672]{0,1:T(8,128)(2,1)} %collective-permute-done.14, bf16[2048,672]{0,1:T(8,128)(2,1)} %collective-permute-done.13, bf16[2048,672]{0,1:T(8,128)(2,1)} %collective-permute-done.12, ...), kind=kLoop, calls=%fused_computation.43 | loop fusion | flops 23396352 | bytes 24772612 | tf_op jit(solution)/shard_map/transpose | solution.py:173
  (86 shorter events, 16.9 us)
Async XLA Ops:
  0.6 31.5 %collective-permute-start = (bf16[512,1344]{0,1:T(8,128)(2,1)}, bf16[512,1344]{0,1:T(8,128)(2,1)S(1)}, u32[]{:S(2)}, u32[]{:S(2)}) collective-permute-start(bf16[512,1344]{0,1:T(8,128)(2,1)} %param.6), channel_id=1, source_target_pairs={{0,1},{1,2},{2,3},{3,0},{4,5},{5,6},{6,7},{7,4},{8,9},{9,10},{10,1... | collective-permute-start | bytes 4128776 | tf_op jit(solution)/shard_map/ppermute | solution.py:24
  0.7 60.7 %collective-permute-start.1 = (bf16[512,1344]{0,1:T(8,128)(2,1)}, bf16[512,1344]{0,1:T(8,128)(2,1)}, u32[]{:S(2)}, u32[]{:S(2)}) collective-permute-start(bf16[512,1344]{0,1:T(8,128)(2,1)} %param.6), channel_id=1, source_target_pairs={{0,3},{1,0},{2,1},{3,2},{4,7},{5,4},{6,5},{7,6},{8,11},{9,8},{10,9... | collective-permute-start | bytes 4128776 | tf_op jit(solution)/shard_map/ppermute | solution.py:27
  32.2 57.4 %collective-permute-start.2 = (bf16[512,1344]{0,1:T(8,128)(2,1)S(1)}, bf16[512,1344]{0,1:T(8,128)(2,1)}, u32[]{:S(2)}, u32[]{:S(2)}) collective-permute-start(bf16[512,1344]{0,1:T(8,128)(2,1)S(1)} %collective-permute-done), channel_id=1, source_target_pairs={{0,1},{1,2},{2,3},{3,0},{4,5},{5,6},{6,7},{7,4},{8,9},{9,10},{10,1... | collective-permute-start | bytes 4128776 | tf_op jit(solution)/shard_map/ppermute | solution.py:24
  36.9 1.3 copy-start.11
  38.2 52.9 %slice-start = ((s8[5505024]{0:T(1024)(128)(4,1)}), s8[4194304]{0:T(1024)(128)(4,1)S(1)}, s32[]{:S(2)}) async-start(s8[5505024]{0:T(1024)(128)(4,1)} %bitcast.80), calls=%async_computation | async-start | bytes 8388608
  41.0 50.1 %slice-start.1 = ((s8[5505024]{0:T(1024)(128)(4,1)}), s8[1310720]{0:T(1024)(128)(4,1)S(1)}, s32[]{:S(2)}) async-start(s8[5505024]{0:T(1024)(128)(4,1)} %bitcast.80), calls=%async_computation.1 | async-start | bytes 2621440
  89.5 4.7 slice-start.2
  91.2 15.5 %copy-start.3 = (bf16[512,5376]{0,1:T(8,128)(2,1)}, bf16[512,5376]{0,1:T(8,128)(2,1)S(1)}, u32[]{:S(2)}) copy-start(bf16[512,5376]{0,1:T(8,128)(2,1)S(1)} %constant_dynamic-update-slice_fusion) | copy-start | bytes 16515076
  91.2 3.1 slice-start.3
  91.2 15.4 %slice-start.4 = ((s8[11010048]{0:T(1024)(128)(4,1)}), s8[4194304]{0:T(1024)(128)(4,1)S(1)}, s32[]{:S(2)}) async-start(s8[11010048]{0:T(1024)(128)(4,1)} %bitcast.94), calls=%async_computation.4 | async-start | bytes 8388608
  91.2 15.4 %slice-start.5 = ((s8[11010048]{0:T(1024)(128)(4,1)}), s8[4194304]{0:T(1024)(128)(4,1)S(1)}, s32[]{:S(2)}) async-start(s8[11010048]{0:T(1024)(128)(4,1)} %bitcast.94), calls=%async_computation.5 | async-start | bytes 8388608
  94.3 12.4 %slice-start.6 = ((s8[11010048]{0:T(1024)(128)(4,1)}), s8[2621440]{0:T(1024)(128)(4,1)S(1)}, s32[]{:S(2)}) async-start(s8[11010048]{0:T(1024)(128)(4,1)} %bitcast.94), calls=%async_computation.6 | async-start | bytes 5242880
  97.4 26.4 %collective-permute-start.4 = (bf16[2,512,512]{2,1,0:T(8,128)(2,1)S(1)}, bf16[2,512,512]{2,1,0:T(8,128)(2,1)}, u32[]{:S(2)}, u32[]{:S(2)}) collective-permute-start(bf16[2,512,512]{2,1,0:T(8,128)(2,1)S(1)} %pad_maximum_fusion.1), channel_id=1, source_target_pairs={{0,4},{4,8},{8,12},{12,16},{16,20},{20,24},{24,28},{1,5},{5,9},{9,... | collective-permute-start | bytes 3145736 | tf_op jit(solution)/shard_map/ppermute | solution.py:37
  103.5 35.0 %collective-permute-start.3 = (bf16[2,512,512]{2,1,0:T(8,128)(2,1)S(1)}, bf16[2,512,512]{2,1,0:T(8,128)(2,1)}, u32[]{:S(2)}, u32[]{:S(2)}) collective-permute-start(bf16[2,512,512]{2,1,0:T(8,128)(2,1)S(1)} %pad_maximum_fusion.1), channel_id=1, source_target_pairs={{0,8},{4,12},{8,16},{12,20},{16,24},{20,28},{1,9},{5,13},{9,17},{1... | collective-permute-start | bytes 3145736 | tf_op jit(solution)/shard_map/ppermute | solution.py:37
  143.0 17.6 %copy-start.1 = (bf16[1536,4,128,1]{0,2,3,1:T(8,128)(2,1)}, bf16[1536,4,128,1]{0,2,3,1:T(8,128)(2,1)S(1)}, u32[]{:S(2)}) copy-start(bf16[1536,4,128,1]{0,2,3,1:T(8,128)(2,1)S(1)} %copy.63) | copy-start | bytes 4718596
  143.0 4.1 copy-start.4
  143.0 4.0 copy-start.13
  178.1 17.0 %copy-start.2 = (bf16[1536,4,128,1]{0,2,3,1:T(8,128)(2,1)S(1)}, bf16[1536,4,128,1]{0,2,3,1:T(8,128)(2,1)}, u32[]{:S(2)}) copy-start(bf16[1536,4,128,1]{0,2,3,1:T(8,128)(2,1)} %copy-done.1) | copy-start | bytes 4718596
  204.9 11.0 %copy-start = (f32[4,128,1536]{2,1,0:T(8,128)S(1)}, f32[4,128,1536]{2,1,0:T(8,128)}, u32[]{:S(2)}) copy-start(f32[4,128,1536]{2,1,0:T(8,128)} %fusion.13) | copy-start | bytes 9437188
  216.0 8.5 %slice-start.7 = ((s8[11010048]{0:T(1024)(128)(4,1)}), s8[2621440]{0:T(1024)(128)(4,1)S(1)}, s32[]{:S(2)}) async-start(s8[11010048]{0:T(1024)(128)(4,1)} %bitcast.96), calls=%async_computation.7 | async-start | bytes 5242880
  216.0 8.5 %slice-start.8 = ((s8[11010048]{0:T(1024)(128)(4,1)}), s8[4194304]{0:T(1024)(128)(4,1)S(1)}, s32[]{:S(2)}) async-start(s8[11010048]{0:T(1024)(128)(4,1)} %bitcast.96), calls=%async_computation.8 | async-start | bytes 8388608
  216.6 4.4 copy-start.12
  216.8 28.0 %collective-permute-start.6 = (bf16[2,512,512]{1,2,0:T(8,128)(2,1)S(1)}, bf16[2,512,512]{1,2,0:T(8,128)(2,1)S(1)}, u32[]{:S(2)}, u32[]{:S(2)}) collective-permute-start(bf16[2,512,512]{1,2,0:T(8,128)(2,1)S(1)} %get-tuple-element.20), channel_id=1, source_target_pairs={{8,0},{12,4},{16,8},{20,12},{24,16},{28,20},{9,1},{13,5},{17,9},{2... | collective-permute-start | bytes 3145736 | tf_op jit(solution)/shard_map/ppermute | solution.py:37
  219.0 29.5 %collective-permute-start.5 = (bf16[2,512,512]{1,2,0:T(8,128)(2,1)S(1)}, bf16[2,512,512]{1,2,0:T(8,128)(2,1)S(1)}, u32[]{:S(2)}, u32[]{:S(2)}) collective-permute-start(bf16[2,512,512]{1,2,0:T(8,128)(2,1)S(1)} %get-tuple-element.19), channel_id=1, source_target_pairs={{4,0},{8,4},{12,8},{16,12},{20,16},{24,20},{28,24},{5,1},{9,5},{13... | collective-permute-start | bytes 3145736 | tf_op jit(solution)/shard_map/ppermute | solution.py:37
  220.9 3.6 slice-start.9
  255.5 44.4 %collective-permute-start.9 = (bf16[512,1344]{0,1:T(8,128)(2,1)}, bf16[512,1344]{0,1:T(8,128)(2,1)S(1)}, u32[]{:S(2)}, u32[]{:S(2)}) collective-permute-start(bf16[512,1344]{0,1:T(8,128)(2,1)} %fusion.19), channel_id=1, source_target_pairs={{0,1},{1,2},{2,3},{3,0},{4,5},{5,6},{6,7},{7,4},{8,9},{9,10},{10,1... | collective-permute-start | bytes 4128776 | tf_op jit(solution)/shard_map/ppermute | solution.py:156
  276.7 13.7 %copy-start.6 = (f32[512,1344]{0,1:T(8,128)S(1)}, f32[512,1344]{0,1:T(8,128)}, u32[]{:S(2)}) copy-start(f32[512,1344]{0,1:T(8,128)} %fusion.27) | copy-start | bytes 8257540
  289.1 98.3 %collective-permute-start.16 = (bf16[2048,672]{0,1:T(8,128)(2,1)S(1)}, bf16[2048,672]{0,1:T(8,128)(2,1)}, u32[]{:S(2)}, u32[]{:S(2)}) collective-permute-start(bf16[2048,672]{0,1:T(8,128)(2,1)S(1)} %get-tuple-element.13), channel_id=1, source_target_pairs={{0,4},{4,8},{8,12},{12,16},{16,20},{20,24},{24,28},{28,0},{1,5},{5... | collective-permute-start | bytes 8257544 | tf_op jit(solution)/shard_map/ppermute | solution.py:172
  289.2 116.4 %collective-permute-start.15 = (bf16[2048,672]{0,1:T(8,128)(2,1)S(1)}, bf16[2048,672]{0,1:T(8,128)(2,1)}, u32[]{:S(2)}, u32[]{:S(2)}) collective-permute-start(bf16[2048,672]{0,1:T(8,128)(2,1)S(1)} %get-tuple-element.14), channel_id=1, source_target_pairs={{0,8},{4,12},{8,16},{12,20},{16,24},{20,28},{24,0},{28,4},{1,9},{5... | collective-permute-start | bytes 8257544 | tf_op jit(solution)/shard_map/ppermute | solution.py:172
  292.7 2.5 copy-start.5
  295.1 91.4 %collective-permute-start.8 = (bf16[512,1344]{0,1:T(8,128)(2,1)S(1)}, bf16[512,1344]{0,1:T(8,128)(2,1)S(1)}, u32[]{:S(2)}, u32[]{:S(2)}) collective-permute-start(bf16[512,1344]{0,1:T(8,128)(2,1)S(1)} %fusion.18), channel_id=1, source_target_pairs={{0,2},{1,3},{2,0},{3,1},{4,6},{5,7},{6,4},{7,5},{8,10},{9,11},{10,... | collective-permute-start | bytes 4128776 | tf_op jit(solution)/shard_map/ppermute | solution.py:156
  299.6 86.8 %collective-permute-start.7 = (bf16[512,1344]{0,1:T(8,128)(2,1)S(1)}, bf16[512,1344]{0,1:T(8,128)(2,1)S(1)}, u32[]{:S(2)}, u32[]{:S(2)}) collective-permute-start(bf16[512,1344]{0,1:T(8,128)(2,1)S(1)} %fusion.17), channel_id=1, source_target_pairs={{0,3},{1,0},{2,1},{3,2},{4,7},{5,4},{6,5},{7,6},{8,11},{9,8},{10,9... | collective-permute-start | bytes 4128776 | tf_op jit(solution)/shard_map/ppermute | solution.py:156
  299.9 115.5 %collective-permute-start.14 = (bf16[2048,672]{0,1:T(8,128)(2,1)}, bf16[2048,672]{0,1:T(8,128)(2,1)}, u32[]{:S(2)}, u32[]{:S(2)}) collective-permute-start(bf16[2048,672]{0,1:T(8,128)(2,1)} %get-tuple-element.15), channel_id=1, source_target_pairs={{0,12},{4,16},{8,20},{12,24},{16,28},{20,0},{24,4},{28,8},{1,13},{... | collective-permute-start | bytes 8257544 | tf_op jit(solution)/shard_map/ppermute | solution.py:172
  386.4 19.2 %copy-start.7 = (bf16[512,1344]{0,1:T(8,128)(2,1)}, bf16[512,1344]{0,1:T(8,128)(2,1)S(1)}, u32[]{:S(2)}) copy-start(bf16[512,1344]{0,1:T(8,128)(2,1)S(1)} %collective-permute-done.8) | copy-start | bytes 4128772
  386.4 179.0 %collective-permute-start.13 = (bf16[2048,672]{0,1:T(8,128)(2,1)}, bf16[2048,672]{0,1:T(8,128)(2,1)}, u32[]{:S(2)}, u32[]{:S(2)}) collective-permute-start(bf16[2048,672]{0,1:T(8,128)(2,1)} %get-tuple-element.16), channel_id=1, source_target_pairs={{0,16},{4,20},{8,24},{12,28},{16,0},{20,4},{24,8},{28,12},{1,17},{... | collective-permute-start | bytes 8257544 | tf_op jit(solution)/shard_map/ppermute | solution.py:172
  386.5 19.2 %copy-start.9 = (bf16[512,1344]{0,1:T(8,128)(2,1)}, bf16[512,1344]{0,1:T(8,128)(2,1)S(1)}, u32[]{:S(2)}) copy-start(bf16[512,1344]{0,1:T(8,128)(2,1)S(1)} %collective-permute-done.7) | copy-start | bytes 4128772
  386.5 209.2 %collective-permute-start.12 = (bf16[2048,672]{0,1:T(8,128)(2,1)}, bf16[2048,672]{0,1:T(8,128)(2,1)}, u32[]{:S(2)}, u32[]{:S(2)}) collective-permute-start(bf16[2048,672]{0,1:T(8,128)(2,1)} %get-tuple-element.17), channel_id=1, source_target_pairs={{0,20},{4,24},{8,28},{12,0},{16,4},{20,8},{24,12},{28,16},{1,21},{... | collective-permute-start | bytes 8257544 | tf_op jit(solution)/shard_map/ppermute | solution.py:172
  387.4 208.2 %collective-permute-start.11 = (bf16[2048,672]{0,1:T(8,128)(2,1)}, bf16[2048,672]{0,1:T(8,128)(2,1)}, u32[]{:S(2)}, u32[]{:S(2)}) collective-permute-start(bf16[2048,672]{0,1:T(8,128)(2,1)} %get-tuple-element.18), channel_id=1, source_target_pairs={{0,24},{4,28},{8,0},{12,4},{16,8},{20,12},{24,16},{28,20},{1,25},{... | collective-permute-start | bytes 8257544 | tf_op jit(solution)/shard_map/ppermute | solution.py:172
  405.6 190.0 %collective-permute-start.10 = (bf16[2048,672]{0,1:T(8,128)(2,1)}, bf16[2048,672]{0,1:T(8,128)(2,1)}, u32[]{:S(2)}, u32[]{:S(2)}) collective-permute-start(bf16[2048,672]{0,1:T(8,128)(2,1)} %get-tuple-element.12), channel_id=1, source_target_pairs={{0,28},{4,0},{8,4},{12,8},{16,12},{20,16},{24,20},{28,24},{1,29},{... | collective-permute-start | bytes 8257544 | tf_op jit(solution)/shard_map/ppermute | solution.py:172
  409.3 2.4 copy-start.8
  409.3 2.4 copy-start.10
